TPU v7x, 512 devices: a whole 4x4x16 slice. The times are simulated.
512 devices in a mesh: front: 4 (over y), row: 4 (over x), col: 32 (over z, core).
Axes of the slice: x: 4, y: 4, z: 16, core: 2. Of those that a mesh axis runs over, the one named last changes fastest.
Arguments:
- inverse_factor: bfloat16 [4, 1024, 1024], P('front', ('row', 'col')), as said below
- panel: bfloat16 [4, 8192, 1024], P('front', 'row', 'col'), may hold values from -1.1953125 to 1.1953125
- trailing: float32 [4, 8192, 8192], P('front', 'row', 'col'), may hold values from -6 to 6
- extend_map: int32 [4, 512], P('front'), may hold values from 0 to 511, as said below
Outputs:
- parent_update: float32 [4, 4096, 8192], P('front', 'row', 'col')
Inputs may be any that keep to these rules, and one draw needn't show every extreme that they name: Each inverse_factor[f] is upper triangular with positive diagonal. Each row of extend_map is a permutation of 0 to 511, and extend_map[f, q] % (128) == q % 128.
All inputs are finite; a program needn't handle non-finite values.
Results may differ from a plain program's by a relative error of at most 0.0034.
Values may be sent and summed in bfloat16 or wider, within the bound.
No kernel may reach another device: no remote copies, remote signals or barrier semaphores. Data moves between devices by JAX's collectives and lax.ppermute only.
A program may use at most 64 MiB of HBM per device.

v0:
```python
import jax
import jax.numpy as jnp
from jax import lax
from jax.sharding import Mesh
from jax.sharding import PartitionSpec as P


def from_partner(value, axis, distance):
    mask = 2**distance
    pairs = [(source, source ^ mask) for source in range(lax.axis_size(axis))]
    return lax.ppermute(value, axis, pairs)


def outer_rows(left, right):
    return lax.dot_general(
        left, right, (((1,), (1,)), ((), ())), preferred_element_type=jnp.float32
    )


def local(inverse_factor, panel, trailing, extend_map):
    nrow = lax.axis_size("row")
    nz = lax.axis_size("z")
    ncore = lax.axis_size("core")
    ncol = nz * ncore
    group = nrow * ncol
    row_index = lax.axis_index("row")
    col_index = lax.axis_index("z") * ncore + lax.axis_index("core")
    inverse = lax.all_gather(inverse_factor[0], "core", axis=0, tiled=True)
    inverse = lax.all_gather(inverse, "z", axis=0, tiled=True)
    inverse = lax.all_gather(inverse, "row", axis=0, tiled=True)
    order = inverse.shape[0]
    chunk = order // ncol
    inverse = inverse.reshape(nz, ncore, chunk, order).transpose(1, 0, 2, 3).reshape(order, order)
    columns = lax.all_gather(panel[0], "z", axis=1, tiled=True)
    columns = lax.all_gather(columns, "core", axis=1, tiled=True)
    solved = jnp.dot(columns, inverse, preferred_element_type=jnp.float32).astype(jnp.bfloat16)
    local_trailing = trailing[0]
    rows_here = local_trailing.shape[0]
    cols_here = local_trailing.shape[1]
    share = rows_here // ncol
    piece = lax.dynamic_slice_in_dim(solved, col_index * share, share, 0)
    col_side = lax.all_gather(piece, "row", axis=0, tiled=True)
    block_map = extend_map[0]
    nblocks = block_map.shape[0]
    per_class = nblocks // group
    width = rows_here // (ncol * per_class)
    slots_row = jnp.arange(ncol * per_class, dtype=jnp.int32)
    class_row = slots_row // per_class
    depth_row = slots_row % per_class
    source_row = (depth_row * ncol + class_row) * nrow + row_index
    target_row = class_row * per_class + block_map[source_row] // group
    gather_row = jnp.argsort(target_row)
    slots_col = jnp.arange(nrow * per_class, dtype=jnp.int32)
    class_col = slots_col // per_class
    depth_col = slots_col % per_class
    source_col = (depth_col * ncol + col_index) * nrow + class_col
    target_col = class_col * per_class + block_map[source_col] // group
    gather_col = jnp.argsort(target_col)
    col_side = col_side.reshape(nrow * per_class, width, order)[gather_col].reshape(
        cols_here, order
    )
    lane = jnp.arange(cols_here, dtype=jnp.int32)
    picked = gather_col[lane // width] * width + lane % width
    select_cols = (lane[:, None] == picked[None, :]).astype(jnp.float32)
    member = lax.axis_index("front") % 2
    half = rows_here // 2
    half_blocks = half // width

    def half_update(which):
        rows = lax.dynamic_slice_in_dim(local_trailing, which * half, half, 0)
        low = lax.dynamic_slice_in_dim(solved, which * half, half, 0)
        moved_cols = jnp.dot(
            rows, select_cols, precision=lax.Precision.HIGHEST, preferred_element_type=jnp.float32
        )
        schur = moved_cols - outer_rows(low, col_side)
        blocks = (
            lax.dynamic_slice_in_dim(gather_row, which * half_blocks, half_blocks, 0)
            - which * half_blocks
        )
        return schur.reshape(half_blocks, width, cols_here)[blocks].reshape(half, cols_here)

    outgoing = half_update(1 - member)
    incoming = from_partner(outgoing, "front", 0)
    keep = half_update(member)
    return (keep + incoming)[None]


def solution(mesh):
    devices = mesh.devices
    shape = devices.shape
    fine = Mesh(
        devices.reshape(shape[0], shape[1], shape[2] // 2, 2), ("front", "row", "z", "core")
    )
    cols = ("z", "core")
    return jax.shard_map(
        local,
        mesh=fine,
        in_specs=(
            P("front", ("row",) + cols, None),
            P("front", "row", cols),
            P("front", "row", cols),
            P("front", None),
        ),
        out_specs=P("front", "row", cols),
        check_vma=False,
    )
```

profile of v0, /device:TPU:8, one launch (start us, length us, event | category | flops | bytes accessed | tf_op | source)
XLA Modules:
  0.0 213.7 jit_solution(8595470988300910653)
XLA Ops:
  6.5 0.0 copy-start
  6.5 0.0 copy-start.1
  6.5 0.0 all-gather.9.cloned.1.call-start
  6.5 0.7 all-gather.9.cloned.1.call-update
  7.3 0.0 all-gather.13.cloned.1.call-start
  7.3 2.0 all-gather.2
  9.3 42.3 %all-gather.3 = bf16[1,256,1024]{2,1,0:T(8,128)(2,1)} all-gather(bf16[1,16,1024]{2,1,0:T(8,128)(2,1)S(1)} %all-gather.2), channel_id=5, replica_groups=mesh['front'=4,'row'=4,'z'=16,'core'=2] {'z'}, dimensions={1}, use_global_device_ids=true | all-gather | bytes 557056 | tf_op jit(solution)/shard_map/all_gather | solution.py:29
  51.6 0.0 all-gather.13.cloned.1.call-update
  51.7 0.0 all-gather.11.cloned.1.call-start
  51.7 35.8 %all-gather.9.cloned.1.call-done = bf16[1,2048,512]{1,2,0:T(8,128)(2,1)} async-done(((bf16[1,2048,32]{1,2,0:T(8,128)(2,1)}), bf16[1,2048,512]{1,2,0:T(8,128)(2,1)}) %all-gather.9.cloned.1.call-update) | async-done | bytes 2097168 | tf_op jit(solution)/shard_map/all_gather | solution.py:34
  87.5 0.0 all-gather.11.cloned.1.call-update
  87.5 0.0 copy-done.1
  87.6 0.7 gather_fusion
  88.2 1.3 gather_fusion.2
  89.6 1.2 sort.34
  90.8 2.5 %sort.35 = (s32[128]{0:T(128)}, s32[128]{0:T(128)S(1)}) sort(s32[128]{0:T(128)S(1)} %fusion.28, s32[128]{0:T(128)S(1)} %iota.41), dimensions={0}, to_apply=%region_1.2 | sort | flops 896 | bytes 2048 | tf_op jit(solution)/shard_map/jit(argsort)/sort | solution.py:52
  93.5 0.1 compare_select_fusion.8
  93.6 0.7 fusion.34
  94.3 4.2 %compare_select_fusion.1 = s32[256,1]{0,1:T(1,128)S(1)} fusion(s32[]{:T(128)} %bitcast.12, s32[]{:T(128)} %bitcast.13, s32[]{:T(128)} %bitcast.14, s32[]{:T(128)} %bitcast.15, s32[]{:T(128)} %bitcast.16, s32[]{:T(128)} %bitcast.18, s32[]{:T(128)} %bitcast.17), kind=kLoop, calls=%fused_computation.37 | loop fusion | flops 5888 | bytes 1052 | tf_op jit(solution)/shard_map/gather | solution.py:63
  98.5 5.6 %fusion.19 = s32[256]{0:T(256)S(1)} fusion(pred[256]{0:T(512)(128)(4,1)S(1)} %get-tuple-element.27, pred[256]{0:T(512)(128)(4,1)S(1)} %get-tuple-element.28, pred[256]{0:T(512)(128)(4,1)S(1)} %get-tuple-element.29, pred[256]{0:T(512)(128)(4,1)S(1)} %get-tuple-element.30, pred[256]{0:T(512)(128)(4,1)S(1)} %get-tuple-element.31, ...), kind=kLoop, calls=%fused_computation.72 | loop fusion | flops 4352 | bytes 4388 | tf_op jit(solution)/shard_map/add | solution.py:63
  104.1 21.1 %all-gather.13.cloned.1.call-done = bf16[1,1024,1024]{2,1,0:T(8,128)(2,1)} async-done(((bf16[1,256,1024]{2,1,0:T(8,128)(2,1)}), bf16[1,1024,1024]{2,1,0:T(8,128)(2,1)}) %all-gather.13.cloned.1.call-update) | async-done | bytes 2097168 | tf_op jit(solution)/shard_map/all_gather | solution.py:30
  125.2 3.3 %copy.5 = bf16[2,16,32,1024]{3,2,1,0:T(8,128)(2,1)} copy(bf16[2,16,32,1024]{3,2,0,1:T(8,128)(2,1)} %bitcast.54) | data formatting | bytes 4194304 | tf_op jit(solution)/shard_map/transpose | solution.py:33
  128.4 23.1 %all-gather.11.cloned.1.call-done = bf16[1,2048,1024]{1,2,0:T(8,128)(2,1)} async-done(((bf16[1,2048,512]{1,2,0:T(8,128)(2,1)}), bf16[1,2048,1024]{1,2,0:T(8,128)(2,1)}) %all-gather.11.cloned.1.call-update) | async-done | bytes 4194320 | tf_op jit(solution)/shard_map/all_gather | solution.py:35
  151.5 7.4 %fusion.2 = bf16[2048,1024]{1,0:T(8,128)(2,1)S(1)} fusion(bf16[1024,1024]{1,0:T(8,128)(2,1)} %bitcast.55, bf16[1,2048,1024]{1,2,0:T(8,128)(2,1)} %all-gather.11.cloned.1.call-done), kind=kOutput, calls=%fused_computation.7 | convolution fusion | flops 4297064448 | bytes 10485760 | tf_op jit(solution)/shard_map/dot_general | solution.py:36
  159.0 0.0 copy-start.2
  159.0 13.1 %all_gather.23 = bf16[256,1024]{1,0:T(8,128)(2,1)S(1)} all-gather(bf16[64,1024]{1,0:T(8,128)(2,1)S(1)} %constant_dynamic-slice_fusion), channel_id=1, replica_groups=mesh['front'=4,'row'=4,'z'=16,'core'=2] {'row'}, dimensions={0}, use_global_device_ids=true | all-gather | bytes 655360 | tf_op jit(solution)/shard_map/all_gather | solution.py:42
  172.1 0.0 copy-done.2
  172.1 0.6 gather_fusion.1
  172.7 2.3 %fusion.5 = f32[1024,256]{1,0:T(8,128)S(1)} fusion(bf16[256,1024]{1,0:T(8,128)(2,1)S(1)} %bitcast.50, bf16[2048,1024]{1,0:T(8,128)(2,1)} %copy-done.2, s32[]{:T(128)S(6)} %select_n.164), kind=kOutput, calls=%fused_computation.8 | convolution fusion | flops 536870912 | bytes 3670020 | tf_op jit(solution)/shard_map/dot_general | solution.py:15
  175.1 0.0 copy-done
  175.1 1.6 convolution_subtract_fusion
  176.7 2.8 %gather_fusion.4 = f32[64,16,256]{2,1,0:T(8,128)} fusion(f32[64,16,256]{2,1,0:T(8,128)} %bitcast.53, s32[1024]{0:T(1024)S(1)} %pad_clamp_fusion), kind=kCustom, calls=%fused_computation.4 | custom fusion | bytes 2097408 | tf_op jit(solution)/shard_map/gather | solution.py:80
  179.5 3.1 %collective-permute-start = (f32[1024,256]{1,0:T(8,128)}, f32[1024,256]{1,0:T(8,128)}, u32[]{:S(2)}, u32[]{:S(2)}) collective-permute-start(f32[1024,256]{1,0:T(8,128)} %bitcast.57), channel_id=1, source_target_pairs={{0,128},{128,0},{256,384},{384,256},{1,129},{129,1},{257,385},{385... | collective-permute-start | bytes 3145736 | tf_op jit(solution)/shard_map/ppermute | solution.py:11
  182.7 2.3 %fusion.7 = f32[1024,256]{1,0:T(8,128)S(1)} fusion(bf16[256,1024]{1,0:T(8,128)(2,1)S(1)} %bitcast.51, bf16[2048,1024]{1,0:T(8,128)(2,1)} %copy-done.2, s32[]{:T(128)S(6)} %select_n.146), kind=kOutput, calls=%fused_computation.10 | convolution fusion | flops 536870912 | bytes 3670020 | tf_op jit(solution)/shard_map/dot_general | solution.py:15
  185.0 1.6 convolution_subtract_fusion.1
  186.6 1.8 gather_fusion.3
  188.5 16.4 %collective-permute-done = f32[1024,256]{1,0:T(8,128)} collective-permute-done((f32[1024,256]{1,0:T(8,128)}, f32[1024,256]{1,0:T(8,128)}, u32[]{:S(2)}, u32[]{:S(2)}) %collective-permute-start) | collective-permute-done | bytes 1048608 | tf_op jit(solution)/shard_map/ppermute | solution.py:11
  204.9 2.3 %bitcast_add_fusion = f32[1024,256]{1,0:T(8,128)} fusion(f32[1024,256]{1,0:T(8,128)} %collective-permute-done, f32[64,16,256]{2,1,0:T(8,128)S(1)} %gather_fusion.3), kind=kLoop, calls=%fused_computation.15 | loop fusion | flops 262144 | bytes 3145728 | tf_op jit(solution)/shard_map/add | solution.py:85
  (18 shorter events, 0.2 us)
Async XLA Ops:
  6.5 168.5 %copy-start = (f32[1,2048,256]{2,1,0:T(8,128)S(1)}, f32[1,2048,256]{2,1,0:T(8,128)}, u32[]{:S(2)}) copy-start(f32[1,2048,256]{2,1,0:T(8,128)} %param.6) | copy-start | bytes 6291460
  6.5 81.0 %copy-start.1 = (s32[1,512]{1,0:T(1,128)S(1)}, s32[1,512]{1,0:T(1,128)}, u32[]{:S(2)}) copy-start(s32[1,512]{1,0:T(1,128)} %param.7) | copy-start | bytes 6148
  6.5 80.9 %all-gather.9.cloned.1.call-start = ((), (), s32[]{:S(2)}) async-start(), calls=%async_computation | async-start | bytes 2228224 | tf_op jit(solution)/shard_map/all_gather | solution.py:34
  7.3 117.9 %all-gather.13.cloned.1.call-start = ((), (), s32[]{:S(2)}) async-start(), calls=%async_computation.2 | async-start | bytes 2621440 | tf_op jit(solution)/shard_map/all_gather | solution.py:30
  51.7 99.9 %all-gather.11.cloned.1.call-start = ((), (), s32[]{:S(2)}) async-start(), calls=%async_computation.1 | async-start | bytes 6291456 | tf_op jit(solution)/shard_map/all_gather | solution.py:35
  159.0 13.2 %copy-start.2 = (bf16[2048,1024]{1,0:T(8,128)(2,1)}, bf16[2048,1024]{1,0:T(8,128)(2,1)S(1)}, u32[]{:S(2)}) copy-start(bf16[2048,1024]{1,0:T(8,128)(2,1)S(1)} %fusion.2) | copy-start | bytes 12582916
  179.5 25.4 %collective-permute-start = (f32[1024,256]{1,0:T(8,128)}, f32[1024,256]{1,0:T(8,128)}, u32[]{:S(2)}, u32[]{:S(2)}) collective-permute-start(f32[1024,256]{1,0:T(8,128)} %bitcast.57), channel_id=1, source_target_pairs={{0,128},{128,0},{256,384},{384,256},{1,129},{129,1},{257,385},{385... | collective-permute-start | bytes 3145736 | tf_op jit(solution)/shard_map/ppermute | solution.py:11
Sparse Core Ops, SparseCore 0:
  9.4 77.9 all-gather.8
  89.6 35.5 all-gather.12
  127.2 24.2 all-gather.10
where the time goes:
time: 214 us
  waiting for transfers between devices  97.1 us (45%)
  blocking collectives  57.4 us (27%)
  other arithmetic  16.1 us (8%)
  matrix products  15.4 us (7%)
  between operations  13.3 us (6%)
  local copies, waits for them, and re-layouts  11.2 us (5%)
  starting transfers between devices  3.22 us (2%)
    all_gather x1, blocking collectives, local(): inverse = lax.all_gather(inverse, 'z', axis=0, tiled=True)  42.3 us
    all_gather x1, waiting for transfers between devices, local(): columns = lax.all_gather(panel[0], 'z', axis=1, tiled=True)  35.8 us
    all_gather x1, waiting for transfers between devices, local(): columns = lax.all_gather(columns, 'core', axis=1, tiled=True)  23.1 us
    all_gather x1, waiting for transfers between devices, local(): inverse = lax.all_gather(inverse, 'row', axis=0, tiled=True)  21.1 us
    ppermute x1, waiting for transfers between devices, from_partner(): return lax.ppermute(value, axis, pairs)  16.4 us
    all_gather x1, blocking collectives, local(): col_side = lax.all_gather(piece, 'row', axis=0, tiled=True)  13.1 us
    dot_general x1, matrix products, local(): jnp.dot(columns, inverse, preferred_element_type=jnp.float32)  7.43 us
    add x1, other arithmetic, local(): picked = gather_col[lane // width] * width + lane % width  5.58 us
  transfers between devices with their start and end apart: 4, of which 4 were waited for; matrix products, arithmetic and copies ran while one was open for 12% of the time, Pallas kernels for 0%

commit v1 on v0

--- a/solution.py
+++ b/solution.py
@@ -31,7 +31,9 @@
     order = inverse.shape[0]
     chunk = order // ncol
     inverse = inverse.reshape(nz, ncore, chunk, order).transpose(1, 0, 2, 3).reshape(order, order)
-    columns = lax.all_gather(panel[0], "z", axis=1, tiled=True)
+    columns = jnp.concatenate(
+        lax.all_to_all(jnp.stack([panel[0]] * lax.axis_size("z")), "z", 0, 0), axis=1
+    )
     columns = lax.all_gather(columns, "core", axis=1, tiled=True)
     solved = jnp.dot(columns, inverse, preferred_element_type=jnp.float32).astype(jnp.bfloat16)
     local_trailing = trailing[0]

time: 214 us -> 273 us (1.28)
  blocking collectives: 57.4 us -> 135 us
  waiting for transfers between devices: 97.1 us -> 60.3 us
  starting transfers between devices: 3.22 us -> 18.6 us
    all_gather x1, blocking collectives: 42.3 us -> 120 us  [local(): inverse = lax.all_gather(inverse, 'z', axis=0, tiled=True)]
    all_gather x1 -> x0, waiting for transfers between devices: 35.8 us -> none  [local(): columns = lax.all_gather(panel[0], 'z', axis=1, tiled=True)]
    all_to_all x0 -> x1, starting transfers between devices: none -> 15.4 us  [local(): lax.all_to_all(jnp.stack([panel[0]] * lax.axis_size('z')), 'z', 0, 0)]
  transfers between devices with their start and end apart: 4 -> 4, of which waited for: 4 -> 3; matrix products, arithmetic and copies ran while one was open for 12% -> 9% of each run, Pallas kernels for 0% -> 0%
where the time goes in v1:
time: 273 us
  blocking collectives  135 us (49%)
  waiting for transfers between devices  60.3 us (22%)
  starting transfers between devices  18.6 us (7%)
  other arithmetic  16.1 us (6%)
  matrix products  15.4 us (6%)
  local copies, waits for them, and re-layouts  13.8 us (5%)
  between operations  13.7 us (5%)
    all_gather x1, blocking collectives, local(): inverse = lax.all_gather(inverse, 'z', axis=0, tiled=True)  120 us
    all_gather x1, waiting for transfers between devices, local(): columns = lax.all_gather(columns, 'core', axis=1, tiled=True)  23.1 us
    all_gather x1, waiting for transfers between devices, local(): inverse = lax.all_gather(inverse, 'row', axis=0, tiled=True)  20.1 us
    ppermute x1, waiting for transfers between devices, from_partner(): return lax.ppermute(value, axis, pairs)  16.4 us
    all_to_all x1, starting transfers between devices, local(): lax.all_to_all(jnp.stack([panel[0]] * lax.axis_size('z')), 'z', 0, 0)  15.4 us
    all_gather x1, blocking collectives, local(): col_side = lax.all_gather(piece, 'row', axis=0, tiled=True)  13.1 us
    dot_general x1, matrix products, local(): jnp.dot(columns, inverse, preferred_element_type=jnp.float32)  7.43 us
    add x1, other arithmetic, local(): picked = gather_col[lane // width] * width + lane % width  5.58 us
  transfers between devices with their start and end apart: 4, of which 3 were waited for; matrix products, arithmetic and copies ran while one was open for 9% of the time, Pallas kernels for 0%

profile of v1, /device:TPU:8, one launch (start us, length us, event | category | flops | bytes accessed | tf_op | source)
XLA Modules:
  0.0 272.7 jit_solution(5347156305078598061)
XLA Ops:
  6.5 0.0 copy-start
  6.5 2.7 stack.3
  9.2 0.0 copy-start.3
  9.2 15.4 %all-to-all-start = ((bf16[16,2048,32]{1,2,0:T(8,128)(2,1)}), bf16[16,2048,32]{1,2,0:T(8,128)(2,1)}, u32[]{:S(2)}, u32[]{:S(2)}) async-start(bf16[16,2048,32]{1,2,0:T(8,128)(2,1)} %stack.3), calls=%async_computation | async-start | bytes 4194304 | tf_op jit(solution)/shard_map/all_to_all | solution.py:35
  24.6 0.0 copy-start.1
  24.6 0.0 all-gather.8.cloned.1.call-start
  24.6 0.0 copy-done.3
  24.7 1.8 all-gather
  26.5 119.8 %all-gather.1 = bf16[1,256,1024]{2,1,0:T(8,128)(2,1)} all-gather(bf16[1,16,1024]{2,1,0:T(8,128)(2,1)S(1)} %all-gather), channel_id=3, replica_groups=mesh['front'=4,'row'=4,'z'=16,'core'=2] {'z'}, dimensions={1}, use_global_device_ids=true | all-gather | bytes 557056 | tf_op jit(solution)/shard_map/all_gather | solution.py:29
  146.3 0.0 all-gather.8.cloned.1.call-update
  146.3 0.0 all-gather.6.cloned.1.call-start
  146.4 0.0 all-to-all-done
  146.4 0.7 all-gather.6.cloned.1.call-update
  147.2 0.0 copy-done.1
  147.2 0.7 gather_fusion
  147.9 1.3 gather_fusion.2
  149.2 1.2 sort.34
  150.4 2.5 sort.35
  153.1 0.1 compare_select_fusion.8
  153.2 0.7 fusion.29
  153.9 4.2 %compare_select_fusion.1 = s32[256,1]{0,1:T(1,128)S(1)} fusion(s32[]{:T(128)} %bitcast.12, s32[]{:T(128)} %bitcast.13, s32[]{:T(128)} %bitcast.14, s32[]{:T(128)} %bitcast.15, s32[]{:T(128)} %bitcast.16, s32[]{:T(128)} %bitcast.18, s32[]{:T(128)} %bitcast.17), kind=kLoop, calls=%fused_computation.35 | loop fusion | flops 5888 | bytes 1052 | tf_op jit(solution)/shard_map/gather | solution.py:65
  158.1 5.6 %fusion.14 = s32[256]{0:T(256)S(1)} fusion(pred[256]{0:T(512)(128)(4,1)S(1)} %get-tuple-element.27, pred[256]{0:T(512)(128)(4,1)S(1)} %get-tuple-element.28, pred[256]{0:T(512)(128)(4,1)S(1)} %get-tuple-element.29, pred[256]{0:T(512)(128)(4,1)S(1)} %get-tuple-element.30, pred[256]{0:T(512)(128)(4,1)S(1)} %get-tuple-element.31, ...), kind=kLoop, calls=%fused_computation.70 | loop fusion | flops 4352 | bytes 4388 | tf_op jit(solution)/shard_map/add | solution.py:65
  163.7 20.1 %all-gather.8.cloned.1.call-done = bf16[1,1024,1024]{2,1,0:T(8,128)(2,1)} async-done(((bf16[1,256,1024]{2,1,0:T(8,128)(2,1)}), bf16[1,1024,1024]{2,1,0:T(8,128)(2,1)}) %all-gather.8.cloned.1.call-update) | async-done | bytes 2097168 | tf_op jit(solution)/shard_map/all_gather | solution.py:30
  183.8 3.3 %copy.6 = bf16[2,16,32,1024]{3,2,1,0:T(8,128)(2,1)} copy(bf16[2,16,32,1024]{3,2,0,1:T(8,128)(2,1)} %bitcast.54) | data formatting | bytes 4194304 | tf_op jit(solution)/shard_map/transpose | solution.py:33
  187.1 23.1 %all-gather.6.cloned.1.call-done = bf16[2048,1024]{0,1:T(8,128)(2,1)} async-done(((bf16[2048,512]{0,1:T(8,128)(2,1)}), bf16[2048,1024]{0,1:T(8,128)(2,1)}) %all-gather.6.cloned.1.call-update) | async-done | bytes 4194320 | tf_op jit(solution)/shard_map/all_gather | solution.py:37
  210.2 7.4 %convolution_convert_fusion = bf16[2048,1024]{1,0:T(8,128)(2,1)S(1)} fusion(bf16[2048,1024]{0,1:T(8,128)(2,1)} %all-gather.6.cloned.1.call-done, bf16[1024,1024]{1,0:T(8,128)(2,1)} %bitcast.55), kind=kOutput, calls=%fused_computation.5 | convolution fusion | flops 4297064448 | bytes 10485760 | tf_op jit(solution)/shard_map/dot_general | solution.py:38
  217.6 0.0 copy-start.2
  217.7 13.1 %all_gather.19 = bf16[256,1024]{1,0:T(8,128)(2,1)S(1)} all-gather(bf16[64,1024]{1,0:T(8,128)(2,1)S(1)} %constant_dynamic-slice_fusion), channel_id=1, replica_groups=mesh['front'=4,'row'=4,'z'=16,'core'=2] {'row'}, dimensions={0}, use_global_device_ids=true | all-gather | bytes 655360 | tf_op jit(solution)/shard_map/all_gather | solution.py:44
  230.8 0.0 copy-done.2
  230.8 0.6 gather_fusion.1
  231.4 2.3 fusion
  233.7 0.0 copy-done
  233.7 1.6 convolution_subtract_fusion
  235.3 2.8 %gather_fusion.4 = f32[64,16,256]{2,1,0:T(8,128)} fusion(f32[64,16,256]{2,1,0:T(8,128)} %bitcast.53, s32[1024]{0:T(1024)S(1)} %pad_clamp_fusion), kind=kCustom, calls=%fused_computation.4 | custom fusion | bytes 2097408 | tf_op jit(solution)/shard_map/gather | solution.py:82
  238.2 3.1 %collective-permute-start = (f32[1024,256]{1,0:T(8,128)}, f32[1024,256]{1,0:T(8,128)}, u32[]{:S(2)}, u32[]{:S(2)}) collective-permute-start(f32[1024,256]{1,0:T(8,128)} %bitcast.57), channel_id=1, source_target_pairs={{0,128},{128,0},{256,384},{384,256},{1,129},{129,1},{257,385},{385... | collective-permute-start | bytes 3145736 | tf_op jit(solution)/shard_map/ppermute | solution.py:11
  241.3 2.3 fusion.2
  243.7 1.6 convolution_subtract_fusion.1
  245.3 1.8 gather_fusion.3
  247.1 16.4 %collective-permute-done = f32[1024,256]{1,0:T(8,128)} collective-permute-done((f32[1024,256]{1,0:T(8,128)}, f32[1024,256]{1,0:T(8,128)}, u32[]{:S(2)}, u32[]{:S(2)}) %collective-permute-start) | collective-permute-done | bytes 1048608 | tf_op jit(solution)/shard_map/ppermute | solution.py:11
  263.5 2.3 bitcast_add_fusion
  (18 shorter events, 0.2 us)
Async XLA Ops:
  6.5 227.2 %copy-start = (f32[1,2048,256]{2,1,0:T(8,128)S(1)}, f32[1,2048,256]{2,1,0:T(8,128)}, u32[]{:S(2)}) copy-start(f32[1,2048,256]{2,1,0:T(8,128)} %param.6) | copy-start | bytes 6291460
  9.2 15.5 %copy-start.3 = (bf16[1,8,1024]{2,1,0:T(8,128)(2,1)S(1)}, bf16[1,8,1024]{2,1,0:T(8,128)(2,1)}, u32[]{:S(2)}) copy-start(bf16[1,8,1024]{2,1,0:T(8,128)(2,1)} %param.4) | copy-start | bytes 49156
  9.2 137.2 %all-to-all-start = ((bf16[16,2048,32]{1,2,0:T(8,128)(2,1)}), bf16[16,2048,32]{1,2,0:T(8,128)(2,1)}, u32[]{:S(2)}, u32[]{:S(2)}) async-start(bf16[16,2048,32]{1,2,0:T(8,128)(2,1)} %stack.3), calls=%async_computation | async-start | bytes 4194304 | tf_op jit(solution)/shard_map/all_to_all | solution.py:35
  24.6 122.6 %copy-start.1 = (s32[1,512]{1,0:T(1,128)S(1)}, s32[1,512]{1,0:T(1,128)}, u32[]{:S(2)}) copy-start(s32[1,512]{1,0:T(1,128)} %param.7) | copy-start | bytes 6148
  24.6 159.2 %all-gather.8.cloned.1.call-start = ((), (), s32[]{:S(2)}) async-start(), calls=%async_computation.2 | async-start | bytes 2621440 | tf_op jit(solution)/shard_map/all_gather | solution.py:30
  146.3 63.8 %all-gather.6.cloned.1.call-start = ((), (), s32[]{:S(2)}) async-start(), calls=%async_computation.1 | async-start | bytes 6291456 | tf_op jit(solution)/shard_map/all_gather | solution.py:37
  217.6 13.2 %copy-start.2 = (bf16[2048,1024]{1,0:T(8,128)(2,1)}, bf16[2048,1024]{1,0:T(8,128)(2,1)S(1)}, u32[]{:S(2)}) copy-start(bf16[2048,1024]{1,0:T(8,128)(2,1)S(1)} %convolution_convert_fusion) | copy-start | bytes 12582916
  238.2 25.4 %collective-permute-start = (f32[1024,256]{1,0:T(8,128)}, f32[1024,256]{1,0:T(8,128)}, u32[]{:S(2)}, u32[]{:S(2)}) collective-permute-start(f32[1024,256]{1,0:T(8,128)} %bitcast.57), channel_id=1, source_target_pairs={{0,128},{128,0},{256,384},{384,256},{1,129},{129,1},{257,385},{385... | collective-permute-start | bytes 3145736 | tf_op jit(solution)/shard_map/ppermute | solution.py:11
Sparse Core Ops, SparseCore 0:
  146.5 37.2 all-gather.7
  185.9 24.2 all-gather.5
